TPU v7x, 256 devices: a whole 4x4x8 slice. The times are simulated.
256 devices in a mesh: gy: 8 (over y, x_hi), gx: 4 (over x_lo, core), wa: 8 (over z).
Axes of the slice: x: 4 (x_hi: 2, x_lo: 2; x = x_hi * 2 + x_lo), y: 4, z: 8, core: 2. Of those that a mesh axis runs over, the one named last changes fastest.
Arguments:
- tokens: bfloat16 [8, 64, 128, 3072], P('wa', 'gy', 'gx'), may hold values from -6 to 6
- mod_shift: float32 [8, 3072], P('wa'), may hold values from -3 to 3
- mod_scale: float32 [8, 3072], P('wa'), may hold values from -0.9 to 3.9
- qkv_weight: bfloat16 [3072, 4608], P(None, ('gx', 'wa')), may hold values from -0.14433757 to 0.14433757
- block_codes: int32 [8, 16, 9], P('gy', 'gx'), may hold values from 0 to 8, as said below
- block_counts: int32 [8, 16], P('gy', 'gx'), may hold values from 1 to 9, as said below
- valid_tokens: int32 [8, 16], replicated, may hold values from 1 to 64
Outputs:
- attended: bfloat16 [8, 64, 128, 1536], P('wa', 'gy', 'gx')
Inputs may be any that keep to these rules, and one draw needn't show every extreme that they name: `block_codes`: the 9 codes of a block's list are distinct, the first is 4 (the block itself), and the first block_counts entries name blocks inside the grid. `block_counts`: A count never exceeds the number of blocks of the 3 x 3 neighbourhood that lie inside the grid.
All inputs are finite; a program needn't handle non-finite values.
Results may differ from a plain program's by a relative error of at most 0.007.
Values may be sent and summed in bfloat16 or wider, within the bound.
No kernel may reach another device: no remote copies, remote signals or barrier semaphores. Data moves between devices by JAX's collectives and lax.ppermute only.
A program may use at most 128 MiB of HBM per device.

v0:
```python
import math
import jax
import jax.numpy as jnp
from jax import lax
from jax.sharding import PartitionSpec as P

D = 3072
HEADS = 12
HD = 128
BLK = 8
NBR = 9


def extended_2(array, sides, width):
    for axis, dim in sides:
        size, length = (lax.axis_size(axis), array.shape[dim])
        up = [(i, (i + 1) % size) for i in range(size - 1)]
        down = [(j, i) for i, j in up]
        last = lax.slice_in_dim(array, length - width, length, axis=dim)
        first = lax.slice_in_dim(array, 0, width, axis=dim)
        before = lax.ppermute(last, axis, up)
        after = lax.ppermute(first, axis, down)
        array = jnp.concatenate([before, array, after], axis=dim)
    return array


def normalize(rows, shift_row, scale_row):
    widened = rows.astype(jnp.float32)
    average = jnp.mean(widened, axis=-1, keepdims=True)
    centred = widened - average
    spread = jnp.mean(centred * centred, axis=-1, keepdims=True)
    return (centred * lax.rsqrt(spread + 1e-06) * (1.0 + scale_row) + shift_row).astype(
        jnp.bfloat16
    )


def to_blocks(field):
    height, breadth, channels = field.shape
    shaped = field.reshape(height // BLK, BLK, breadth // BLK, BLK, channels)
    return shaped.transpose(0, 2, 1, 3, 4).reshape(
        height // BLK, breadth // BLK, BLK * BLK, channels
    )


def from_blocks(blocks):
    block_rows, block_cols, cells, channels = blocks.shape
    shaped = blocks.reshape(block_rows, block_cols, BLK, BLK, channels)
    return shaped.transpose(0, 2, 1, 3, 4).reshape(block_rows * BLK, block_cols * BLK, channels)


def make_mask(counts, live_count):
    slot_ids = jnp.arange(NBR, dtype=jnp.int32)
    token_ids = jnp.arange(BLK * BLK, dtype=jnp.int32)
    used = slot_ids[:, None] < counts[..., None, None]
    return used & (token_ids < live_count[..., None])


def attend(queries, key_blocks, key_mask):
    number = queries.shape[0]
    query_heads = queries.reshape(number, BLK * BLK, HEADS, HD)
    key_value = key_blocks.reshape(number, NBR * BLK * BLK, 2, HEADS, HD)
    scores = jnp.einsum(
        "nqhd,nkhd->nhqk", query_heads, key_value[:, :, 0], preferred_element_type=jnp.float32
    ) * (1.0 / math.sqrt(HD))
    scores = jnp.where(key_mask[:, None, None, :], scores, -jnp.inf)
    highest = jnp.max(scores, axis=-1, keepdims=True)
    exponent = jnp.exp(scores - highest)
    probs = (exponent / jnp.sum(exponent, axis=-1, keepdims=True)).astype(jnp.bfloat16)
    blended = jnp.einsum(
        "nhqk,nkhd->nqhd", probs, key_value[:, :, 1], preferred_element_type=jnp.float32
    )
    return blended.astype(jnp.bfloat16).reshape(number, BLK * BLK, HEADS * HD)


def body(tokens, mod_shift, mod_scale, qkv_weight, block_codes, block_counts, valid_tokens):
    tile_rows = tokens.shape[1]
    tile_cols = tokens.shape[2]
    width = HEADS * HD
    weight_block = lax.all_gather(qkv_weight, "wa", axis=1, tiled=True)
    flat_rows = normalize(tokens[0], mod_shift[0], mod_scale[0]).reshape(tile_rows * tile_cols, D)
    row_group = lax.all_gather(flat_rows, "gx", axis=0, tiled=True)
    partial = jnp.dot(row_group, weight_block, preferred_element_type=jnp.float32).astype(
        jnp.bfloat16
    )
    qkv = lax.all_to_all(partial, "gx", 0, 1, tiled=True)
    qkv_grid = qkv.reshape(tile_rows, tile_cols, 3 * width)
    extended = extended_2(qkv_grid[:, :, width:], (("gy", 0), ("gx", 1)), BLK)
    block_rows = tile_rows // BLK
    block_cols = tile_cols // BLK
    queries = to_blocks(qkv_grid[:, :, :width])
    key_blocks = to_blocks(extended)
    row_ids = jnp.arange(block_rows, dtype=jnp.int32)[:, None, None]
    col_ids = jnp.arange(block_cols, dtype=jnp.int32)[None, :, None]
    row_step = block_codes // 3 - 1
    col_step = block_codes % 3 - 1
    picked = key_blocks[row_ids + 1 + row_step, col_ids + 1 + col_step]
    global_row = jnp.clip(
        lax.axis_index("gy") * block_rows + row_ids + row_step, 0, valid_tokens.shape[0] - 1
    )
    global_col = jnp.clip(
        lax.axis_index("gx") * block_cols + col_ids + col_step, 0, valid_tokens.shape[1] - 1
    )
    live_count = valid_tokens[global_row, global_col]
    key_mask = make_mask(block_counts, live_count)
    number = block_rows * block_cols
    result = attend(
        queries.reshape(number, BLK * BLK, width),
        picked.reshape(number, NBR, BLK * BLK, 2 * width),
        key_mask.reshape(number, NBR * BLK * BLK),
    )
    return from_blocks(result.reshape(block_rows, block_cols, BLK * BLK, width))[None]


def solution(mesh):
    return jax.shard_map(
        body,
        mesh=mesh,
        in_specs=(
            P("wa", "gy", "gx", None),
            P("wa", None),
            P("wa", None),
            P(None, ("gx", "wa")),
            P("gy", "gx", None),
            P("gy", "gx"),
            P(),
        ),
        out_specs=P("wa", "gy", "gx", None),
        check_vma=False,
    )
```

profile of v0, /device:TPU:25, one launch (start us, length us, event | category | flops | bytes accessed | tf_op | source)
XLA Modules:
  0.0 396.4 jit_solution(5357344674858160736)
XLA Ops:
  6.5 0.0 copy-start
  6.5 0.0 all-gather.3.cloned.1.call-start
  6.5 1.7 convert_reduce_fusion
  8.3 0.1 div.23
  8.3 2.0 fusion.8
  10.3 0.1 rsqrt.12
  10.4 0.7 broadcast_add_fusion
  11.1 3.3 fusion.12
  14.4 0.0 all-gather.3.cloned.1.call-update
  14.5 0.0 all-gather.5.cloned.1.call-start
  14.5 0.7 all-gather.5.cloned.1.call-update
  15.2 69.0 %all-gather.3.cloned.1.call-done = bf16[1024,3072]{1,0:T(8,128)(2,1)} async-done(((bf16[256,3072]{1,0:T(8,128)(2,1)}), bf16[1024,3072]{1,0:T(8,128)(2,1)}) %all-gather.3.cloned.1.call-update) | async-done | bytes 6291472 | tf_op jit(solution)/shard_map/all_gather | solution.py:81
  84.2 83.9 %all-gather.5.cloned.1.call-done = bf16[3072,1152]{0,1:T(8,128)(2,1)} async-done(((bf16[3072,144]{0,1:T(8,128)(2,1)}), bf16[3072,1152]{0,1:T(8,128)(2,1)}) %all-gather.5.cloned.1.call-update) | async-done | bytes 7077904 | tf_op jit(solution)/shard_map/all_gather | solution.py:79
  168.2 12.5 %convolution_convert_fusion = bf16[1024,1152]{1,0:T(8,128)(2,1)S(1)} fusion(bf16[1024,3072]{1,0:T(8,128)(2,1)} %all-gather.3.cloned.1.call-done, bf16[3072,1152]{0,1:T(8,128)(2,1)} %all-gather.5.cloned.1.call-done), kind=kOutput, calls=%fused_computation.16 | convolution fusion | flops 7248936960 | bytes 15728640 | tf_op jit(solution)/shard_map/dot_general | solution.py:82
  180.7 30.8 %all_to_all.16 = bf16[4,256,1152]{2,1,0:T(8,128)(2,1)S(1)} all-to-all(bf16[4,256,1152]{2,1,0:T(8,128)(2,1)S(1)} %bitcast.72), channel_id=1, replica_groups=mesh['gy'=8,'gx'=4,'wa'=8] {'gx'}, dimensions={0} | all-to-all | bytes 4718592 | tf_op jit(solution)/shard_map/all_to_all | solution.py:85
  211.5 1.8 copy.23
  213.3 0.0 copy-start.3
  213.3 2.4 reshape.129
  215.7 1.6 slice.31
  217.3 0.0 copy-start.4
  217.3 4.8 %collective-permute-start.1 = (bf16[8,32,3072]{2,1,0:T(8,128)(2,1)S(1)}, bf16[8,32,3072]{2,1,0:T(8,128)(2,1)S(1)}, u32[]{:S(2)}, u32[]{:S(2)}) collective-permute-start(bf16[8,32,3072]{2,1,0:T(8,128)(2,1)S(1)} %slice.31), channel_id=1, source_target_pairs={{32,0},{64,32},{96,64},{128,96},{160,128},{192,160},{224,192},{33,... | collective-permute-start | bytes 4718600 | tf_op jit(solution)/shard_map/ppermute | solution.py:22
  222.1 2.1 collective-permute-start
  224.2 0.0 copy-done.3
  224.2 0.1 fusion.19
  224.3 31.3 %collective-permute-done.1 = bf16[8,32,3072]{2,1,0:T(8,128)(2,1)S(1)} collective-permute-done((bf16[8,32,3072]{2,1,0:T(8,128)(2,1)S(1)}, bf16[8,32,3072]{2,1,0:T(8,128)(2,1)S(1)}, u32[]{:S(2)}, u32[]{:S(2)}) %collective-permute-start.1) | collective-permute-done | bytes 1572896 | tf_op jit(solution)/shard_map/ppermute | solution.py:22
  255.6 34.1 %collective-permute-done = bf16[8,32,3072]{2,1,0:T(8,128)(2,1)} collective-permute-done((bf16[8,32,3072]{2,1,0:T(8,128)(2,1)S(1)}, bf16[8,32,3072]{2,1,0:T(8,128)(2,1)}, u32[]{:S(2)}, u32[]{:S(2)}) %collective-permute-start) | collective-permute-done | bytes 1572896 | tf_op jit(solution)/shard_map/ppermute | solution.py:21
  289.7 2.8 pad_maximum_fusion.3
  292.4 4.3 %collective-permute-start.2 = (bf16[24,8,3072]{2,1,0:T(8,128)(2,1)}, bf16[24,8,3072]{2,1,0:T(8,128)(2,1)}, u32[]{:S(2)}, u32[]{:S(2)}) collective-permute-start(bf16[24,8,3072]{2,1,0:T(8,128)(2,1)} %get-tuple-element.7), channel_id=1, source_target_pairs={{0,8},{8,16},{16,24},{1,9},{9,17},{17,25},{2,10},{10,18},{18,26},{... | collective-permute-start | bytes 3538952 | tf_op jit(solution)/shard_map/ppermute | solution.py:21
  296.7 2.1 collective-permute-start.3
  298.8 0.1 reshape.144
  298.9 0.0 copy-done
  298.9 0.9 gather_fusion.1
  299.8 0.1 lt.77
  299.9 0.1 reshape.136
  299.9 0.0 copy-done.4
  299.9 0.1 iota_compare_fusion
  300.0 0.1 and.28
  300.1 0.1 and.29
  300.2 0.1 lt.73
  300.3 0.1 lt.78
  300.3 0.1 lt.79
  300.4 2.1 copy_bitcast_fusion.10
  302.5 2.4 reshape_reshape_reshape.6
  304.9 5.2 %collective-permute-done.2 = bf16[24,8,3072]{2,1,0:T(8,128)(2,1)} collective-permute-done((bf16[24,8,3072]{2,1,0:T(8,128)(2,1)}, bf16[24,8,3072]{2,1,0:T(8,128)(2,1)}, u32[]{:S(2)}, u32[]{:S(2)}) %collective-permute-start.2) | collective-permute-done | bytes 1179680 | tf_op jit(solution)/shard_map/ppermute | solution.py:21
  310.1 4.4 %collective-permute-done.3 = bf16[24,8,3072]{2,1,0:T(8,128)(2,1)} collective-permute-done((bf16[24,8,3072]{2,1,0:T(8,128)(2,1)}, bf16[24,8,3072]{2,1,0:T(8,128)(2,1)}, u32[]{:S(2)}, u32[]{:S(2)}) %collective-permute-start.3) | collective-permute-done | bytes 1179680 | tf_op jit(solution)/shard_map/ppermute | solution.py:22
  314.5 3.3 pad_maximum_fusion
  317.8 3.7 copy.46
  321.6 10.6 %gather_fusion = bf16[36,64,3072]{2,1,0:T(8,128)(2,1)} fusion(bf16[3,6,64,3072]{3,2,1,0:T(8,128)(2,1)} %bitcast.69, s32[36]{0:T(128)S(1)} %reshape.136), kind=kCustom, calls=%fused_computation | custom fusion | bytes 28311840 | tf_op jit(solution)/shard_map/gather | solution.py:96
  332.1 25.4 %reshape_reshape.3 = bf16[4,576,2,12,128]{4,3,2,1,0:T(8,128)(2,1)} reshape(bf16[36,64,3072]{2,1,0:T(8,128)(2,1)} %gather_fusion) | data formatting | bytes 28311552 | tf_op jit(solution)/shard_map/reshape;reshape | solution.py:61
  357.5 0.0 copy-start.2
  357.5 12.5 %fusion.30 = (bf16[4,576,1,12,128]{4,3,2,1,0:T(8,128)(2,1)S(1)}, bf16[4,576,1,12,128]{4,3,2,1,0:T(8,128)(2,1)}) fusion(bf16[4,576,2,12,128]{4,3,2,1,0:T(8,128)(2,1)} %reshape_reshape.3), kind=kLoop, calls=%fused_computation.70 | loop fusion | bytes 28311552 | tf_op jit(solution)/shard_map/slice | solution.py:63
  370.1 0.0 copy-done.2
  370.1 3.4 fusion.2
  373.5 4.4 %fusion.31 = (f32[4,12,64]{2,1,0:T(8,128)S(1)}, f32[4,12,64,576]{3,2,1,0:T(8,128)}) fusion(f32[4,12,64,576]{3,2,1,0:T(8,128)S(1)} %fusion.2, pred[4,576]{1,0:T(4,128)(4,1)S(1)} %compare_and_fusion), kind=kOutput, calls=%fused_computation.71 | output fusion | flops 10617407 | bytes 14170368 | tf_op jit(solution)/shard_map/sub | solution.py:67
  377.9 0.0 copy-start.1
  377.9 9.6 %fusion.14 = bf16[4,64,12,128]{3,1,2,0:T(8,128)(2,1)S(1)} fusion(bf16[4,576,1,12,128]{4,3,2,1,0:T(8,128)(2,1)} %get-tuple-element.6, f32[4,12,64,576]{3,2,1,0:T(8,128)} %get-tuple-element.14, f32[4,12,64]{2,1,0:T(8,128)S(1)} %get-tuple-element.13), kind=kOutput, calls=%fused_computation.27 | convolution fusion | flops 456916992 | bytes 14954496 | tf_op jit(solution)/shard_map/nhqk,nkhd->nqhd/dot_general | solution.py:69
  387.5 0.5 copy.29
  388.1 0.5 reshape_reshape_reshape.7
  388.6 0.9 copy_bitcast_fusion.9
  389.6 0.0 copy-done.1
  (9 shorter events, 0.1 us)
Async XLA Ops:
  6.5 292.4 %copy-start = (s32[8,16]{1,0:T(8,128)S(1)}, s32[8,16]{1,0:T(8,128)}, u32[]{:S(2)}) copy-start(s32[8,16]{1,0:T(8,128)} %param.13) | copy-start | bytes 1540
  6.5 77.7 %all-gather.3.cloned.1.call-start = ((), (), s32[]{:S(2)}) async-start(), calls=%async_computation.1 | async-start | bytes 7864320 | tf_op jit(solution)/shard_map/all_gather | solution.py:81
  14.5 153.7 %all-gather.5.cloned.1.call-start = ((), (), s32[]{:S(2)}) async-start(), calls=%async_computation.2 | async-start | bytes 7962624 | tf_op jit(solution)/shard_map/all_gather | solution.py:79
  213.3 10.9 %copy-start.3 = (s32[1,4,9]{2,1,0:T(4,128)S(1)}, s32[1,4,9]{2,1,0:T(4,128)}, u32[]{:S(2)}) copy-start(s32[1,4,9]{2,1,0:T(4,128)} %param.11) | copy-start | bytes 436
  217.3 82.7 %copy-start.4 = (s32[1,4]{1,0:T(1,128)S(1)}, s32[1,4]{1,0:T(1,128)}, u32[]{:S(2)}) copy-start(s32[1,4]{1,0:T(1,128)} %param.12) | copy-start | bytes 52
  217.3 38.3 %collective-permute-start.1 = (bf16[8,32,3072]{2,1,0:T(8,128)(2,1)S(1)}, bf16[8,32,3072]{2,1,0:T(8,128)(2,1)S(1)}, u32[]{:S(2)}, u32[]{:S(2)}) collective-permute-start(bf16[8,32,3072]{2,1,0:T(8,128)(2,1)S(1)} %slice.31), channel_id=1, source_target_pairs={{32,0},{64,32},{96,64},{128,96},{160,128},{192,160},{224,192},{33,... | collective-permute-start | bytes 4718600 | tf_op jit(solution)/shard_map/ppermute | solution.py:22
  222.1 67.6 %collective-permute-start = (bf16[8,32,3072]{2,1,0:T(8,128)(2,1)S(1)}, bf16[8,32,3072]{2,1,0:T(8,128)(2,1)}, u32[]{:S(2)}, u32[]{:S(2)}) collective-permute-start(bf16[8,32,3072]{2,1,0:T(8,128)(2,1)S(1)} %slice.31), channel_id=1, source_target_pairs={{0,32},{32,64},{64,96},{96,128},{128,160},{160,192},{192,224},{1,3... | collective-permute-start | bytes 4718600 | tf_op jit(solution)/shard_map/ppermute | solution.py:21
  292.4 17.7 %collective-permute-start.2 = (bf16[24,8,3072]{2,1,0:T(8,128)(2,1)}, bf16[24,8,3072]{2,1,0:T(8,128)(2,1)}, u32[]{:S(2)}, u32[]{:S(2)}) collective-permute-start(bf16[24,8,3072]{2,1,0:T(8,128)(2,1)} %get-tuple-element.7), channel_id=1, source_target_pairs={{0,8},{8,16},{16,24},{1,9},{9,17},{17,25},{2,10},{10,18},{18,26},{... | collective-permute-start | bytes 3538952 | tf_op jit(solution)/shard_map/ppermute | solution.py:21
  296.7 17.8 %collective-permute-start.3 = (bf16[24,8,3072]{2,1,0:T(8,128)(2,1)}, bf16[24,8,3072]{2,1,0:T(8,128)(2,1)}, u32[]{:S(2)}, u32[]{:S(2)}) collective-permute-start(bf16[24,8,3072]{2,1,0:T(8,128)(2,1)} %get-tuple-element.8), channel_id=1, source_target_pairs={{8,0},{16,8},{24,16},{9,1},{17,9},{25,17},{10,2},{18,10},{26,18},{... | collective-permute-start | bytes 3538952 | tf_op jit(solution)/shard_map/ppermute | solution.py:22
  357.5 12.5 %copy-start.2 = (bf16[4,64,12,128]{3,2,1,0:T(8,128)(2,1)S(1)}, bf16[4,64,12,128]{3,2,1,0:T(8,128)(2,1)}, u32[]{:S(2)}) copy-start(bf16[4,64,12,128]{3,2,1,0:T(8,128)(2,1)} %reshape_reshape_reshape.6) | copy-start | bytes 2359300
  377.9 11.6 %copy-start.1 = (s32[8,16]{1,0:T(8,128)S(1)}, s32[8,16]{1,0:T(8,128)}, u32[]{:S(2)}) copy-start(s32[8,16]{1,0:T(8,128)} %param.13) | copy-start | bytes 1540
Sparse Core Ops, SparseCore 0:
  14.6 69.5 all-gather.2
  86.0 82.0 all-gather.4
where the time goes:
time: 398 us; the launch traced here: 396 us
  waiting for transfers between devices  229 us (58%)
  local copies, waits for them, and re-layouts  66.2 us (17%)
  blocking collectives  30.8 us (8%)
  matrix products  25.5 us (6%)
  other arithmetic  18.4 us (5%)
  between operations  13.6 us (3%)
  starting transfers between devices  13.3 us (3%)
    all_gather x1, waiting for transfers between devices, body(): weight_block = lax.all_gather(qkv_weight, 'wa', axis=1, tiled=True)  83.9 us
    all_gather x1, waiting for transfers between devices, body(): row_group = lax.all_gather(flat_rows, 'gx', axis=0, tiled=True)  69 us
    ppermute x2, waiting for transfers between devices, extended_2(): before = lax.ppermute(last, axis, up)  39.3 us
    ppermute x2, waiting for transfers between devices, extended_2(): after = lax.ppermute(first, axis, down)  35.7 us
    all_to_all x1, blocking collectives, body(): qkv = lax.all_to_all(partial, 'gx', 0, 1, tiled=True)  30.8 us
    another operation x1, local copies, waits for them, and re-layouts, attend(): key_value = key_blocks.reshape(number, NBR * BLK * BLK, 2, HEADS, HD)  25.4 us
    slice x1, local copies, waits for them, and re-layouts, attend(): key_value[:, :, 0]  12.5 us
    dot_general x1, matrix products, body(): jnp.dot(row_group, weight_block, preferred_element_type=jnp.float32)  12.5 us
  transfers between devices with their start and end apart: 6, of which 6 were waited for; matrix products, arithmetic and copies ran while one was open for 2% of the time, Pallas kernels for 0%

commit v1 on v0

--- a/solution.py
+++ b/solution.py
@@ -76,7 +76,21 @@
     tile_rows = tokens.shape[1]
     tile_cols = tokens.shape[2]
     width = HEADS * HD
-    weight_block = lax.all_gather(qkv_weight, "wa", axis=1, tiled=True)
+    ways, here, step = (lax.axis_size("wa"), lax.axis_index("wa"), qkv_weight.shape[1])
+    shape = [n * ways if d == 1 else n for d, n in enumerate(qkv_weight.shape)]
+    full = lax.dynamic_update_slice_in_dim(
+        jnp.zeros(shape, qkv_weight.dtype), qkv_weight, here * step, axis=1
+    )
+    going_up = going_down = qkv_weight
+    for far in range(1, ways // 2 + 1):
+        going_up = lax.ppermute(going_up, "wa", [(d, (d + 1) % ways) for d in range(ways)])
+        full = lax.dynamic_update_slice_in_dim(full, going_up, (here - far) % ways * step, axis=1)
+        if 2 * far < ways:
+            going_down = lax.ppermute(going_down, "wa", [(d, (d - 1) % ways) for d in range(ways)])
+            full = lax.dynamic_update_slice_in_dim(
+                full, going_down, (here + far) % ways * step, axis=1
+            )
+    weight_block = full
     flat_rows = normalize(tokens[0], mod_shift[0], mod_scale[0]).reshape(tile_rows * tile_cols, D)
     row_group = lax.all_gather(flat_rows, "gx", axis=0, tiled=True)
     partial = jnp.dot(row_group, weight_block, preferred_element_type=jnp.float32).astype(

time: 398 us -> 334 us (0.84)
  waiting for transfers between devices: 229 us -> 138 us
  local copies, waits for them, and re-layouts: 66.2 us -> 79 us
  starting transfers between devices: 13.3 us -> 24.1 us
    all_gather x1 -> x0, waiting for transfers between devices: 83.9 us -> none  [body(): weight_block = lax.all_gather(qkv_weight, 'wa', axis=1, tiled=True)]
    all_gather x1, waiting for transfers between devices: 69 us -> 0.01 us  [body(): row_group = lax.all_gather(flat_rows, 'gx', axis=0, tiled=True)]
    ppermute x0 -> x7, waiting for transfers between devices: none -> 63.2 us  [the longest x4 62.9 us: body(): lax.ppermute(going_up, 'wa', [(d, (d + 1) % ways) for d in range(ways)])]
    ppermute x0 -> x7, starting transfers between devices: none -> 11.1 us  [the longest x3 9.4 us: body(): lax.ppermute(going_down, 'wa', [(d, (d - 1) % ways) for d in range(ways)])]
    dynamic_update_slice x0 -> x8, local copies, waits for them, and re-layouts: none -> 9.07 us  [the longest x4 5.12 us: body(): lax.dynamic_update_slice_in_dim(full, going_up, (here - far) % ways * ste...]
  transfers between devices with their start and end apart: 6 -> 12, of which waited for: 6 -> 9; matrix products, arithmetic and copies ran while one was open for 2% -> 6% of each run, Pallas kernels for 0% -> 0%
where the time goes in v1:
time: 334 us; the launch traced here: 333 us
  waiting for transfers between devices  138 us (41%)
  local copies, waits for them, and re-layouts  79 us (24%)
  blocking collectives  33.8 us (10%)
  matrix products  25.5 us (8%)
  starting transfers between devices  24.1 us (7%)
  other arithmetic  18.5 us (6%)
  between operations  13.6 us (4%)
    ppermute x4, waiting for transfers between devices, body(): lax.ppermute(going_up, 'wa', [(d, (d + 1) % ways) for d in range(ways)])  62.9 us
    ppermute x2, waiting for transfers between devices, extended_2(): before = lax.ppermute(last, axis, up)  39.3 us
    ppermute x2, waiting for transfers between devices, extended_2(): after = lax.ppermute(first, axis, down)  35.7 us
    all_to_all x1, blocking collectives, body(): qkv = lax.all_to_all(partial, 'gx', 0, 1, tiled=True)  33.8 us
    another operation x1, local copies, waits for them, and re-layouts, attend(): key_value = key_blocks.reshape(number, NBR * BLK * BLK, 2, HEADS, HD)  25.4 us
    slice x1, local copies, waits for them, and re-layouts, attend(): key_value[:, :, 0]  12.5 us
    dot_general x1, matrix products, body(): jnp.dot(row_group, weight_block, preferred_element_type=jnp.float32)  12.5 us
    gather x1, local copies, waits for them, and re-layouts, body(): picked = key_blocks[row_ids + 1 + row_step, col_ids + 1 + col_step]  10.5 us
  transfers between devices with their start and end apart: 12, of which 9 were waited for; matrix products, arithmetic and copies ran while one was open for 6% of the time, Pallas kernels for 0%

profile of v1, /device:TPU:25, one launch (start us, length us, event | category | flops | bytes accessed | tf_op | source)
XLA Modules:
  0.0 332.8 jit_solution(14335047027872870338)
XLA Ops:
  6.5 1.8 convert_reduce_fusion
  8.3 0.1 div.23
  8.4 2.0 fusion.8
  10.4 0.1 rsqrt.12
  10.5 0.7 broadcast_add_fusion
  11.2 3.3 %fusion.12 = bf16[256,3072]{1,0:T(8,128)(2,1)} fusion(bf16[1,8,32,3072]{3,2,1,0:T(8,128)(2,1)} %param.7, f32[3072]{0:T(1024)} %bitcast.74, f32[3072]{0:T(1024)S(1)} %bitcast.73, f32[256]{0:T(256)S(1)} %rsqrt.12, f32[256]{0:T(256)S(1)} %div.23), kind=kLoop, calls=%fused_computation.24 | loop fusion | flops 4718592 | bytes 3172352 | tf_op jit(solution)/shard_map/convert_element_type | solution.py:32
  14.5 0.0 all-gather.2.cloned.1.call-update
  14.5 1.7 collective-permute-start
  16.3 4.0 %collective-permute-start.1 = (bf16[3072,144]{0,1:T(8,128)(2,1)S(1)}, bf16[3072,144]{0,1:T(8,128)(2,1)S(1)}, u32[]{:S(2)}, u32[]{:S(2)}) collective-permute-start(bf16[3072,144]{0,1:T(8,128)(2,1)S(1)} %copy-done.3), channel_id=1, source_target_pairs={{0,7},{1,0},{2,1},{3,2},{4,3},{5,4},{6,5},{7,6},{8,15},{9,8},{10,9... | collective-permute-start | bytes 2654216 | tf_op jit(solution)/shard_map/ppermute | solution.py:89
  20.3 19.4 %collective-permute-done = bf16[3072,144]{0,1:T(8,128)(2,1)} collective-permute-done((bf16[3072,144]{0,1:T(8,128)(2,1)S(1)}, bf16[3072,144]{0,1:T(8,128)(2,1)}, u32[]{:S(2)}, u32[]{:S(2)}) %collective-permute-start) | collective-permute-done | bytes 884768 | tf_op jit(solution)/shard_map/ppermute | solution.py:86
  39.7 0.0 collective-permute-start.2
  39.7 2.7 collective-permute-start.3
  42.3 3.8 %broadcast_in_dim.36 = bf16[3072,1152]{0,1:T(8,128)(2,1)} broadcast(bf16[]{:T(256)} %constant.96.clone.1), dimensions={} | broadcast | bytes 7077890 | tf_op jit(solution)/shard_map/broadcast_in_dim | solution.py:82
  46.1 1.0 constant_dynamic-update-slice_fusion.7
  47.1 13.9 %collective-permute-done.2 = bf16[3072,144]{0,1:T(8,128)(2,1)S(1)} collective-permute-done((bf16[3072,144]{0,1:T(8,128)(2,1)}, bf16[3072,144]{0,1:T(8,128)(2,1)S(1)}, u32[]{:S(2)}, u32[]{:S(2)}) %collective-permute-start.2) | collective-permute-done | bytes 884768 | tf_op jit(solution)/shard_map/ppermute | solution.py:86
  61.0 2.2 constant_dynamic-update-slice_fusion.6
  63.2 1.0 constant_dynamic-update-slice_fusion.5
  64.2 2.7 collective-permute-start.5
  66.9 1.0 constant_dynamic-update-slice_fusion.4
  67.9 13.4 %collective-permute-done.4 = bf16[3072,144]{0,1:T(8,128)(2,1)S(1)} collective-permute-done((bf16[3072,144]{0,1:T(8,128)(2,1)S(1)}, bf16[3072,144]{0,1:T(8,128)(2,1)S(1)}, u32[]{:S(2)}, u32[]{:S(2)}) %collective-permute-start.4) | collective-permute-done | bytes 884768 | tf_op jit(solution)/shard_map/ppermute | solution.py:86
  81.4 1.0 constant_dynamic-update-slice_fusion.3
  82.4 1.0 constant_dynamic-update-slice_fusion.2
  83.3 0.3 collective-permute-done.5
  83.6 1.0 constant_dynamic-update-slice_fusion.1
  84.6 16.2 %collective-permute-done.6 = bf16[3072,144]{0,1:T(8,128)(2,1)S(1)} collective-permute-done((bf16[3072,144]{0,1:T(8,128)(2,1)S(1)}, bf16[3072,144]{0,1:T(8,128)(2,1)S(1)}, u32[]{:S(2)}, u32[]{:S(2)}) %collective-permute-start.6) | collective-permute-done | bytes 884768 | tf_op jit(solution)/shard_map/ppermute | solution.py:86
  100.8 1.0 constant_dynamic-update-slice_fusion
  101.8 12.5 %convolution_convert_fusion = bf16[1024,1152]{1,0:T(8,128)(2,1)S(1)} fusion(bf16[1024,3072]{1,0:T(8,128)(2,1)} %all-gather.2.cloned.1.call-done, bf16[3072,1152]{0,1:T(8,128)(2,1)} %constant_dynamic-update-slice_fusion), kind=kOutput, calls=%fused_computation.16 | convolution fusion | flops 7248936960 | bytes 15728640 | tf_op jit(solution)/shard_map/dot_general | solution.py:96
  114.3 33.8 %all_to_all.16 = bf16[4,256,1152]{2,1,0:T(8,128)(2,1)S(1)} all-to-all(bf16[4,256,1152]{2,1,0:T(8,128)(2,1)S(1)} %bitcast.72), channel_id=1, replica_groups=mesh['gy'=8,'gx'=4,'wa'=8] {'gx'}, dimensions={0} | all-to-all | bytes 4718592 | tf_op jit(solution)/shard_map/all_to_all | solution.py:99
  148.1 1.8 copy.23
  149.9 2.4 reshape.129
  152.3 1.6 slice.31
  153.9 4.8 %collective-permute-start.8 = (bf16[8,32,3072]{2,1,0:T(8,128)(2,1)S(1)}, bf16[8,32,3072]{2,1,0:T(8,128)(2,1)S(1)}, u32[]{:S(2)}, u32[]{:S(2)}) collective-permute-start(bf16[8,32,3072]{2,1,0:T(8,128)(2,1)S(1)} %slice.31), channel_id=1, source_target_pairs={{32,0},{64,32},{96,64},{128,96},{160,128},{192,160},{224,192},{33,... | collective-permute-start | bytes 4718600 | tf_op jit(solution)/shard_map/ppermute | solution.py:22
  158.6 2.1 collective-permute-start.7
  160.8 0.1 fusion.19
  160.9 31.3 %collective-permute-done.8 = bf16[8,32,3072]{2,1,0:T(8,128)(2,1)S(1)} collective-permute-done((bf16[8,32,3072]{2,1,0:T(8,128)(2,1)S(1)}, bf16[8,32,3072]{2,1,0:T(8,128)(2,1)S(1)}, u32[]{:S(2)}, u32[]{:S(2)}) %collective-permute-start.8) | collective-permute-done | bytes 1572896 | tf_op jit(solution)/shard_map/ppermute | solution.py:22
  192.2 34.0 %collective-permute-done.7 = bf16[8,32,3072]{2,1,0:T(8,128)(2,1)} collective-permute-done((bf16[8,32,3072]{2,1,0:T(8,128)(2,1)S(1)}, bf16[8,32,3072]{2,1,0:T(8,128)(2,1)}, u32[]{:S(2)}, u32[]{:S(2)}) %collective-permute-start.7) | collective-permute-done | bytes 1572896 | tf_op jit(solution)/shard_map/ppermute | solution.py:21
  226.2 2.8 pad_maximum_fusion.3
  229.0 4.1 %collective-permute-start.9 = (bf16[24,8,3072]{2,1,0:T(8,128)(2,1)}, bf16[24,8,3072]{2,1,0:T(8,128)(2,1)}, u32[]{:S(2)}, u32[]{:S(2)}) collective-permute-start(bf16[24,8,3072]{2,1,0:T(8,128)(2,1)} %get-tuple-element.7), channel_id=1, source_target_pairs={{0,8},{8,16},{16,24},{1,9},{9,17},{17,25},{2,10},{10,18},{18,26},{... | collective-permute-start | bytes 3538952 | tf_op jit(solution)/shard_map/ppermute | solution.py:21
  233.1 2.0 collective-permute-start.10
  235.1 0.1 reshape.144
  235.2 0.9 gather_fusion.1
  236.1 0.1 lt.146
  236.2 0.1 reshape.136
  236.2 0.1 iota_compare_fusion
  236.3 0.1 and.65
  236.4 0.1 and.66
  236.5 0.1 lt.142
  236.6 0.1 lt.147
  236.6 0.1 lt.148
  236.7 2.1 copy_bitcast_fusion.10
  238.8 2.4 reshape_reshape_reshape.6
  241.2 5.3 %collective-permute-done.9 = bf16[24,8,3072]{2,1,0:T(8,128)(2,1)} collective-permute-done((bf16[24,8,3072]{2,1,0:T(8,128)(2,1)}, bf16[24,8,3072]{2,1,0:T(8,128)(2,1)}, u32[]{:S(2)}, u32[]{:S(2)}) %collective-permute-start.9) | collective-permute-done | bytes 1179680 | tf_op jit(solution)/shard_map/ppermute | solution.py:21
  246.5 4.4 %collective-permute-done.10 = bf16[24,8,3072]{2,1,0:T(8,128)(2,1)} collective-permute-done((bf16[24,8,3072]{2,1,0:T(8,128)(2,1)}, bf16[24,8,3072]{2,1,0:T(8,128)(2,1)}, u32[]{:S(2)}, u32[]{:S(2)}) %collective-permute-start.10) | collective-permute-done | bytes 1179680 | tf_op jit(solution)/shard_map/ppermute | solution.py:22
  250.9 3.3 pad_maximum_fusion
  254.2 3.7 %copy.46 = bf16[3,8,6,8,3072]{4,3,1,2,0:T(8,128)(2,1)} copy(bf16[3,8,6,8,3072]{4,3,2,1,0:T(8,128)(2,1)S(1)} %bitcast.70) | data formatting | bytes 14155776 | tf_op jit(solution)/shard_map/reshape | solution.py:39
  258.0 10.5 %gather_fusion = bf16[36,64,3072]{2,1,0:T(8,128)(2,1)} fusion(bf16[3,6,64,3072]{3,2,1,0:T(8,128)(2,1)} %bitcast.69, s32[36]{0:T(128)S(1)} %reshape.136), kind=kCustom, calls=%fused_computation | custom fusion | bytes 28311840 | tf_op jit(solution)/shard_map/gather | solution.py:110
  268.5 25.4 %reshape_reshape.3 = bf16[4,576,2,12,128]{4,3,2,1,0:T(8,128)(2,1)} reshape(bf16[36,64,3072]{2,1,0:T(8,128)(2,1)} %gather_fusion) | data formatting | bytes 28311552 | tf_op jit(solution)/shard_map/reshape;reshape | solution.py:61
  293.9 12.5 %fusion.30 = (bf16[4,576,1,12,128]{4,3,2,1,0:T(8,128)(2,1)S(1)}, bf16[4,576,1,12,128]{4,3,2,1,0:T(8,128)(2,1)}) fusion(bf16[4,576,2,12,128]{4,3,2,1,0:T(8,128)(2,1)} %reshape_reshape.3), kind=kLoop, calls=%fused_computation.78 | loop fusion | bytes 28311552 | tf_op jit(solution)/shard_map/slice | solution.py:63
  306.5 3.4 %fusion.2 = f32[4,12,64,576]{3,2,1,0:T(8,128)S(1)} fusion(bf16[4,576,1,12,128]{4,3,2,1,0:T(8,128)(2,1)S(1)} %get-tuple-element.5, bf16[4,64,12,128]{3,2,1,0:T(8,128)(2,1)S(1)} %copy-done.2), kind=kOutput, calls=%fused_computation.10 | convolution fusion | flops 452984832 | bytes 14942208 | tf_op jit(solution)/shard_map/nqhd,nkhd->nhqk/dot_general | solution.py:62
  309.9 4.4 %fusion.31 = (f32[4,12,64]{2,1,0:T(8,128)S(1)}, f32[4,12,64,576]{3,2,1,0:T(8,128)}) fusion(f32[4,12,64,576]{3,2,1,0:T(8,128)S(1)} %fusion.2, pred[4,576]{1,0:T(4,128)(4,1)S(1)} %compare_and_fusion), kind=kOutput, calls=%fused_computation.79 | output fusion | flops 10617407 | bytes 14170368 | tf_op jit(solution)/shard_map/sub | solution.py:67
  314.3 9.6 %fusion.14 = bf16[4,64,12,128]{3,1,2,0:T(8,128)(2,1)S(1)} fusion(bf16[4,576,1,12,128]{4,3,2,1,0:T(8,128)(2,1)} %get-tuple-element.6, f32[4,12,64,576]{3,2,1,0:T(8,128)} %get-tuple-element.14, f32[4,12,64]{2,1,0:T(8,128)S(1)} %get-tuple-element.13), kind=kOutput, calls=%fused_computation.27 | convolution fusion | flops 456916992 | bytes 14954496 | tf_op jit(solution)/shard_map/nhqk,nkhd->nqhd/dot_general | solution.py:69
  323.9 0.5 copy.29
  324.4 0.5 reshape_reshape_reshape.7
  325.0 0.9 copy_bitcast_fusion.9
  (27 shorter events, 0.1 us)
Async XLA Ops:
  6.5 228.7 %copy-start = (s32[8,16]{1,0:T(8,128)S(1)}, s32[8,16]{1,0:T(8,128)}, u32[]{:S(2)}) copy-start(s32[8,16]{1,0:T(8,128)} %param.13) | copy-start | bytes 1540
  6.5 8.0 %copy-start.3 = (bf16[3072,144]{0,1:T(8,128)(2,1)S(1)}, bf16[3072,144]{0,1:T(8,128)(2,1)}, u32[]{:S(2)}) copy-start(bf16[3072,144]{0,1:T(8,128)(2,1)} %param.10) | copy-start | bytes 2654212
  6.5 95.2 %all-gather.2.cloned.1.call-start = ((), (), s32[]{:S(2)}) async-start(), calls=%async_computation.1 | async-start | bytes 7864320 | tf_op jit(solution)/shard_map/all_gather | solution.py:95
  14.5 25.1 %collective-permute-start = (bf16[3072,144]{0,1:T(8,128)(2,1)S(1)}, bf16[3072,144]{0,1:T(8,128)(2,1)}, u32[]{:S(2)}, u32[]{:S(2)}) collective-permute-start(bf16[3072,144]{0,1:T(8,128)(2,1)S(1)} %copy-done.3), channel_id=1, source_target_pairs={{0,1},{1,2},{2,3},{3,4},{4,5},{5,6},{6,7},{7,0},{8,9},{9,10},{10,1... | collective-permute-start | bytes 2654216 | tf_op jit(solution)/shard_map/ppermute | solution.py:86
  16.3 23.4 %collective-permute-start.1 = (bf16[3072,144]{0,1:T(8,128)(2,1)S(1)}, bf16[3072,144]{0,1:T(8,128)(2,1)S(1)}, u32[]{:S(2)}, u32[]{:S(2)}) collective-permute-start(bf16[3072,144]{0,1:T(8,128)(2,1)S(1)} %copy-done.3), channel_id=1, source_target_pairs={{0,7},{1,0},{2,1},{3,2},{4,3},{5,4},{6,5},{7,6},{8,15},{9,8},{10,9... | collective-permute-start | bytes 2654216 | tf_op jit(solution)/shard_map/ppermute | solution.py:89
  39.7 21.4 %collective-permute-start.2 = (bf16[3072,144]{0,1:T(8,128)(2,1)}, bf16[3072,144]{0,1:T(8,128)(2,1)S(1)}, u32[]{:S(2)}, u32[]{:S(2)}) collective-permute-start(bf16[3072,144]{0,1:T(8,128)(2,1)} %collective-permute-done), channel_id=1, source_target_pairs={{0,1},{1,2},{2,3},{3,4},{4,5},{5,6},{6,7},{7,0},{8,9},{9,10},{10,1... | collective-permute-start | bytes 2654216 | tf_op jit(solution)/shard_map/ppermute | solution.py:86
  39.7 24.6 %collective-permute-start.3 = (bf16[3072,144]{0,1:T(8,128)(2,1)S(1)}, bf16[3072,144]{0,1:T(8,128)(2,1)S(1)}, u32[]{:S(2)}, u32[]{:S(2)}) collective-permute-start(bf16[3072,144]{0,1:T(8,128)(2,1)S(1)} %collective-permute-done.1), channel_id=1, source_target_pairs={{0,7},{1,0},{2,1},{3,2},{4,3},{5,4},{6,5},{7,6},{8,15},{9,8},{10,9... | collective-permute-start | bytes 2654216 | tf_op jit(solution)/shard_map/ppermute | solution.py:89
  61.0 20.3 %collective-permute-start.4 = (bf16[3072,144]{0,1:T(8,128)(2,1)S(1)}, bf16[3072,144]{0,1:T(8,128)(2,1)S(1)}, u32[]{:S(2)}, u32[]{:S(2)}) collective-permute-start(bf16[3072,144]{0,1:T(8,128)(2,1)S(1)} %collective-permute-done.2), channel_id=1, source_target_pairs={{0,1},{1,2},{2,3},{3,4},{4,5},{5,6},{6,7},{7,0},{8,9},{9,10},{10,1... | collective-permute-start | bytes 2654216 | tf_op jit(solution)/shard_map/ppermute | solution.py:86
  64.2 19.4 %collective-permute-start.5 = (bf16[3072,144]{0,1:T(8,128)(2,1)S(1)}, bf16[3072,144]{0,1:T(8,128)(2,1)S(1)}, u32[]{:S(2)}, u32[]{:S(2)}) collective-permute-start(bf16[3072,144]{0,1:T(8,128)(2,1)S(1)} %collective-permute-done.3), channel_id=1, source_target_pairs={{0,7},{1,0},{2,1},{3,2},{4,3},{5,4},{6,5},{7,6},{8,15},{9,8},{10,9... | collective-permute-start | bytes 2654216 | tf_op jit(solution)/shard_map/ppermute | solution.py:89
  81.4 19.5 %collective-permute-start.6 = (bf16[3072,144]{0,1:T(8,128)(2,1)S(1)}, bf16[3072,144]{0,1:T(8,128)(2,1)S(1)}, u32[]{:S(2)}, u32[]{:S(2)}) collective-permute-start(bf16[3072,144]{0,1:T(8,128)(2,1)S(1)} %collective-permute-done.4), channel_id=1, source_target_pairs={{0,1},{1,2},{2,3},{3,4},{4,5},{5,6},{6,7},{7,0},{8,9},{9,10},{10,1... | collective-permute-start | bytes 2654216 | tf_op jit(solution)/shard_map/ppermute | solution.py:86
  148.1 12.7 %copy-start.4 = (s32[1,4,9]{2,1,0:T(4,128)S(1)}, s32[1,4,9]{2,1,0:T(4,128)}, u32[]{:S(2)}) copy-start(s32[1,4,9]{2,1,0:T(4,128)} %param.11) | copy-start | bytes 436
  152.3 84.0 %copy-start.5 = (s32[1,4]{1,0:T(1,128)S(1)}, s32[1,4]{1,0:T(1,128)}, u32[]{:S(2)}) copy-start(s32[1,4]{1,0:T(1,128)} %param.12) | copy-start | bytes 52
  153.9 38.3 %collective-permute-start.8 = (bf16[8,32,3072]{2,1,0:T(8,128)(2,1)S(1)}, bf16[8,32,3072]{2,1,0:T(8,128)(2,1)S(1)}, u32[]{:S(2)}, u32[]{:S(2)}) collective-permute-start(bf16[8,32,3072]{2,1,0:T(8,128)(2,1)S(1)} %slice.31), channel_id=1, source_target_pairs={{32,0},{64,32},{96,64},{128,96},{160,128},{192,160},{224,192},{33,... | collective-permute-start | bytes 4718600 | tf_op jit(solution)/shard_map/ppermute | solution.py:22
  158.6 67.5 %collective-permute-start.7 = (bf16[8,32,3072]{2,1,0:T(8,128)(2,1)S(1)}, bf16[8,32,3072]{2,1,0:T(8,128)(2,1)}, u32[]{:S(2)}, u32[]{:S(2)}) collective-permute-start(bf16[8,32,3072]{2,1,0:T(8,128)(2,1)S(1)} %slice.31), channel_id=1, source_target_pairs={{0,32},{32,64},{64,96},{96,128},{128,160},{160,192},{192,224},{1,3... | collective-permute-start | bytes 4718600 | tf_op jit(solution)/shard_map/ppermute | solution.py:21
  229.0 17.6 %collective-permute-start.9 = (bf16[24,8,3072]{2,1,0:T(8,128)(2,1)}, bf16[24,8,3072]{2,1,0:T(8,128)(2,1)}, u32[]{:S(2)}, u32[]{:S(2)}) collective-permute-start(bf16[24,8,3072]{2,1,0:T(8,128)(2,1)} %get-tuple-element.7), channel_id=1, source_target_pairs={{0,8},{8,16},{16,24},{1,9},{9,17},{17,25},{2,10},{10,18},{18,26},{... | collective-permute-start | bytes 3538952 | tf_op jit(solution)/shard_map/ppermute | solution.py:21
  233.1 17.8 %collective-permute-start.10 = (bf16[24,8,3072]{2,1,0:T(8,128)(2,1)}, bf16[24,8,3072]{2,1,0:T(8,128)(2,1)}, u32[]{:S(2)}, u32[]{:S(2)}) collective-permute-start(bf16[24,8,3072]{2,1,0:T(8,128)(2,1)} %get-tuple-element.8), channel_id=1, source_target_pairs={{8,0},{16,8},{24,16},{9,1},{17,9},{25,17},{10,2},{18,10},{26,18},{... | collective-permute-start | bytes 3538952 | tf_op jit(solution)/shard_map/ppermute | solution.py:22
  293.9 12.6 %copy-start.2 = (bf16[4,64,12,128]{3,2,1,0:T(8,128)(2,1)S(1)}, bf16[4,64,12,128]{3,2,1,0:T(8,128)(2,1)}, u32[]{:S(2)}) copy-start(bf16[4,64,12,128]{3,2,1,0:T(8,128)(2,1)} %reshape_reshape_reshape.6) | copy-start | bytes 2359300
  314.3 11.6 %copy-start.1 = (s32[8,16]{1,0:T(8,128)S(1)}, s32[8,16]{1,0:T(8,128)}, u32[]{:S(2)}) copy-start(s32[8,16]{1,0:T(8,128)} %param.13) | copy-start | bytes 1540
Sparse Core Ops, SparseCore 0:
  14.7 69.6 all-gather.1
